TPU v7x, 256 devices: a whole 4x4x8 slice. The times are simulated.
256 devices in a mesh: rep: 32 (over x, y, core), tp: 8 (over z).
Axes of the slice: x: 4, y: 4, z: 8, core: 2. Of those that a mesh axis runs over, the one named last changes fastest.
Arguments:
- prompt_rows: bfloat16 [20480, 2048], P(('rep', 'tp')), may hold values from -6 to 6
- prompt_pieces: int32 [32, 640], P('rep'), may hold values from 0 to 9, never falling along the last dimension, each value on 1 to 320 neighbouring positions
- decode_rows: bfloat16 [1280, 2048], P('rep'), may hold values from -6 to 6
- request_ages: int32 [1280], P('rep'), may hold values from 2 to 127
- migrate_to: int32 [512, 1], P('rep'), may hold values from 0 to 31, as said below
- past_cache: bfloat16 [1280, 2, 128, 2048], P('rep', None, None, 'tp'), may hold values from -8 to 8
- norm_gain: float32 [2048], replicated, may hold values from 0.5 to 1.5
- norm_bias: float32 [2048], replicated, may hold values from -2 to 2
- qkv_weight: bfloat16 [3, 2048, 2048], P(None, None, 'tp'), may hold values from -0.125 to 0.125
- qkv_bias: float32 [3, 2048], P(None, 'tp'), may hold values from -4 to 4
- out_weight: bfloat16 [2048, 2048], P('tp'), may hold values from -0.125 to 0.125
- out_bias: float32 [2048], replicated, may hold values from -3 to 3
Outputs:
- prompt_out: bfloat16 [20480, 2048], P(('rep', 'tp'))
- prompt_cache: bfloat16 [2, 20480, 2048], P(None, 'rep', 'tp')
- kept_out: bfloat16 [768, 2048], P('rep')
- kept_cache: bfloat16 [768, 2, 128, 2048], P('rep', None, None, 'tp')
- moved_out: bfloat16 [1024, 2048], P('rep')
- moved_cache: bfloat16 [1024, 2, 128, 2048], P('rep', None, None, 'tp')
Inputs may be any that keep to these rules, and one draw needn't show every extreme that they name: `migrate_to`: the 16 requests that leave one replica name 16 different target replicas, and one target replica is named by every replica. `prompt_pieces`: piece numbers never fall along a replica's prompt tokens; a piece has at most 320 tokens, and some piece exactly that many.
All inputs are finite; a program needn't handle non-finite values.
Results may differ from a plain program's by a relative error of at most 0.014.
Values may be sent and summed in bfloat16 or wider, within the bound.
No kernel may reach another device: no remote copies, remote signals or barrier semaphores. Data moves between devices by JAX's collectives and lax.ppermute only.
A program may use at most 128 MiB of HBM per device.

v0:
```python
import jax
import jax.numpy as jnp
from jax import lax
from jax.sharding import PartitionSpec as P

HEAD_DIM = 128
CAP = 1
EPSILON = 1e-05


def layer_norm(values, norm_gain, norm_bias):
    wide = values.astype(jnp.float32)
    center = jnp.mean(wide, axis=-1, keepdims=True)
    spread = jnp.mean(jnp.square(wide - center), axis=-1, keepdims=True)
    scaled = (wide - center) * lax.rsqrt(spread + EPSILON)
    return (scaled * norm_gain + norm_bias).astype(jnp.bfloat16)


def decode_partial(
    rows, cache, live, position, norm_gain, norm_bias, qkv_weight, qkv_bias, out_weight
):
    count = rows.shape[0]
    width = qkv_weight.shape[2]
    heads_here = width // HEAD_DIM
    length = cache.shape[2]
    normed = layer_norm(rows, norm_gain, norm_bias)
    projected = jnp.einsum("rd,cde->cre", normed, qkv_weight, preferred_element_type=jnp.float32)
    queries = (projected[0] + qkv_bias[0]).astype(jnp.bfloat16).reshape(count, heads_here, HEAD_DIM)
    key_new = (projected[1] + qkv_bias[1]).astype(jnp.bfloat16)
    value_new = (projected[2] + qkv_bias[2]).astype(jnp.bfloat16)
    old_keys = cache[:, 0].reshape(count, length, heads_here, HEAD_DIM)
    old_values = cache[:, 1].reshape(count, length, heads_here, HEAD_DIM)
    scale = HEAD_DIM ** (-0.5)
    scores = (
        jnp.einsum("rhe,rlhe->rhl", queries, old_keys, preferred_element_type=jnp.float32) * scale
    )
    own = (
        jnp.sum(
            queries.astype(jnp.float32)
            * key_new.astype(jnp.float32).reshape(count, heads_here, HEAD_DIM),
            axis=-1,
        )
        * scale
    )
    scores = jnp.where(live[:, None, :], scores, -1e30)
    highest = jnp.maximum(jnp.max(scores, axis=-1), own)
    weights = jnp.exp(scores - highest[..., None])
    own_weight = jnp.exp(own - highest)
    total = jnp.sum(weights, axis=-1) + own_weight
    probs = (weights / total[..., None]).astype(jnp.bfloat16)
    own_prob = (own_weight / total).astype(jnp.bfloat16)
    context = jnp.einsum("rhl,rlhe->rhe", probs, old_values, preferred_element_type=jnp.float32)
    context = context + own_prob.astype(jnp.float32)[..., None] * value_new.astype(
        jnp.float32
    ).reshape(count, heads_here, HEAD_DIM)
    context = context.reshape(count, width).astype(jnp.bfloat16)
    partial_value = jnp.dot(context, out_weight, preferred_element_type=jnp.float32)
    written = (jnp.arange(length)[None, :] == position[:, None])[:, :, None]
    new_keys = jnp.where(written, key_new[:, None, :], cache[:, 0])
    new_values = jnp.where(written, value_new[:, None, :], cache[:, 1])
    return (partial_value, jnp.stack([new_keys, new_values], axis=1))


def on_device(
    prompt_rows,
    prompt_pieces,
    decode_rows,
    request_ages,
    migrate_to,
    past_cache,
    norm_gain,
    norm_bias,
    qkv_weight,
    qkv_bias,
    out_weight,
    out_bias,
):
    rep_count = lax.axis_size("rep")
    width = qkv_weight.shape[2]
    heads_here = width // HEAD_DIM
    length = past_cache.shape[2]
    leaving = migrate_to.shape[0]
    staying = decode_rows.shape[0] - leaving
    slot_count = rep_count * CAP
    normed = layer_norm(lax.all_gather(prompt_rows, "tp", axis=0, tiled=True), norm_gain, norm_bias)
    projected = jnp.einsum("rd,cde->cre", normed, qkv_weight, preferred_element_type=jnp.float32)
    total_rows = projected.shape[1]
    queries = (projected[0] + qkv_bias[0]).astype(jnp.bfloat16)
    key_rows = (projected[1] + qkv_bias[1]).astype(jnp.bfloat16)
    value_rows = (projected[2] + qkv_bias[2]).astype(jnp.bfloat16)
    head_q = queries.reshape(total_rows, heads_here, HEAD_DIM)
    head_k = key_rows.reshape(total_rows, heads_here, HEAD_DIM)
    head_v = value_rows.reshape(total_rows, heads_here, HEAD_DIM)
    scores = jnp.einsum(
        "qhe,khe->hqk", head_q, head_k, preferred_element_type=jnp.float32
    ) * HEAD_DIM ** (-0.5)
    pieces = prompt_pieces[0]
    position = jnp.arange(total_rows)
    allowed = (pieces[:, None] == pieces[None, :]) & (position[None, :] <= position[:, None])
    scores = jnp.where(allowed[None], scores, -1e30)
    highest = jnp.max(scores, axis=-1, keepdims=True)
    weights = jnp.exp(scores - highest)
    probs = (weights / jnp.sum(weights, axis=-1, keepdims=True)).astype(jnp.bfloat16)
    context = jnp.einsum("hqk,khe->qhe", probs, head_v, preferred_element_type=jnp.float32)
    context = context.reshape(total_rows, width).astype(jnp.bfloat16)
    attended = lax.psum_scatter(
        jnp.dot(context, out_weight, preferred_element_type=jnp.float32).astype(jnp.bfloat16),
        "tp",
        scatter_dimension=0,
        tiled=True,
    ).astype(jnp.float32)
    prompt_out = (prompt_rows.astype(jnp.float32) + attended + out_bias).astype(jnp.bfloat16)
    prompt_cache = jnp.stack([key_rows, value_rows])
    targets = migrate_to[:, 0]
    onehot = (targets[:, None] == jnp.arange(rep_count)[None, :]).astype(jnp.float32)
    lower = (jnp.arange(leaving)[:, None] > jnp.arange(leaving)[None, :]).astype(jnp.float32)
    earlier = jnp.dot(lower, onehot)
    rank = jnp.sum(earlier * onehot, axis=1).astype(jnp.int32)
    slot = targets * CAP + rank
    placing = (jnp.arange(slot_count)[:, None] == slot[None, :]).astype(jnp.bfloat16)
    cells = jnp.arange(length)
    live = cells[None, :] < request_ages[:, None]
    partial_value, updated = decode_partial(
        decode_rows,
        past_cache,
        live,
        request_ages,
        norm_gain,
        norm_bias,
        qkv_weight,
        qkv_bias,
        out_weight,
    )
    summed = lax.psum(partial_value.astype(jnp.bfloat16), "tp").astype(jnp.float32)
    decode_out = (decode_rows.astype(jnp.float32) + summed + out_bias).astype(jnp.bfloat16)
    kept_out = decode_out[:staying]
    kept_cache = updated[:staying]
    send_cache = jnp.einsum(
        "so,oklh->sklh", placing, updated[staying:], preferred_element_type=jnp.float32
    ).astype(jnp.bfloat16)
    send_rows = jnp.dot(placing, decode_out[staying:], preferred_element_type=jnp.float32).astype(
        jnp.bfloat16
    )
    moved_cache, moved_out = (
        lax.all_to_all(send_cache, "rep", split_axis=0, concat_axis=0, tiled=True),
        lax.all_to_all(send_rows, "rep", split_axis=0, concat_axis=0, tiled=True),
    )
    return (prompt_out, prompt_cache, kept_out, kept_cache, moved_out, moved_cache)


def solution(mesh):
    placed = (
        P(("rep", "tp"), None),
        P("rep", None),
        P("rep", None),
        P("rep"),
        P("rep", None),
        P("rep", None, None, "tp"),
        P(),
        P(),
        P(None, None, "tp"),
        P(None, "tp"),
        P("tp", None),
        P(),
    )
    return jax.shard_map(
        on_device,
        mesh=mesh,
        in_specs=placed,
        out_specs=(
            P(("rep", "tp"), None),
            P(None, "rep", "tp"),
            P("rep", None),
            P("rep", None, None, "tp"),
            P("rep", None),
            P("rep", None, None, "tp"),
        ),
        check_vma=False,
    )
```

profile of v0, /device:TPU:8, one launch (start us, length us, event | category | flops | bytes accessed | tf_op | source)
XLA Modules:
  0.0 225.0 jit_solution(8399299144730349695)
XLA Ops:
  7.2 0.7 all-gather.2.cloned.1.call-update
  8.0 0.8 iota_compare_fusion.1
  8.9 1.0 convert_reduce_fusion.1
  10.0 1.1 fusion.32
  11.1 1.6 convolution_bitcast_fusion
  13.1 5.5 %fusion.71 = (bf16[40,1,128,256]{3,2,1,0:T(8,128)(2,1)}, bf16[40,1,128,256]{3,2,1,0:T(8,128)(2,1)}) fusion(bf16[40,2,128,256]{3,2,1,0:T(8,128)(2,1)} %param.17), kind=kLoop, calls=%fused_computation.117 | loop fusion | bytes 10485760 | tf_op jit(solution)/shard_map/slice | solution.py:31
  18.6 4.4 %copy.84 = bf16[40,1,128,256]{2,3,0,1:T(8,128)(2,1)} copy(bf16[40,1,128,256]{3,2,1,0:T(8,128)(2,1)} %get-tuple-element.36) | data formatting | bytes 5242880 | tf_op jit(solution)/shard_map/reshape;squeeze | solution.py:31
  23.0 2.6 %fusion.53 = f32[40,2,1,128]{3,2,1,0:T(1,128)S(1)} fusion(bf16[40,128,2,128]{1,3,2,0:T(8,128)(2,1)} %bitcast.75, bf16[40,2,128,1]{2,1,0,3:T(2,128)(2,1)S(1)} %get-tuple-element.49), kind=kOutput, calls=%fused_computation.82 | convolution fusion | flops 2621440 | bytes 2682880 | tf_op jit(solution)/shard_map/rhe,rlhe->rhl/dot_general | solution.py:35
  26.1 4.9 %reshape.266 = bf16[40,128,2,128]{3,2,1,0:T(2,128)(2,1)} reshape(bf16[40,1,128,256]{3,2,1,0:T(8,128)(2,1)} %get-tuple-element.37) | data formatting | bytes 5242880 | tf_op jit(solution)/shard_map/reshape;squeeze | solution.py:32
  31.1 4.4 %fusion.11 = f32[40,2,1,128]{3,2,1,0:T(1,128)S(1)} fusion(bf16[40,2,128,1]{2,0,1,3:T(8,128)(2,1)S(1)} %fusion.59, bf16[40,128,2,128]{3,2,1,0:T(2,128)(2,1)} %reshape.266), kind=kOutput, calls=%fused_computation.20 | convolution fusion | flops 2621440 | bytes 2682880 | tf_op jit(solution)/shard_map/rhl,rlhe->rhe/dot_general | solution.py:52
  35.7 1.0 convolution_convert_fusion.2
  36.6 0.2 reduce-scatter.2.cloned.1.call-start
  36.9 0.3 fusion.29
  37.2 1.0 fusion.23
  38.3 8.5 %broadcast_select_fusion = (bf16[40,1,128,256]{3,0,2,1:T(8,128)(2,1)}, bf16[40,1,128,256]{3,0,2,1:T(8,128)(2,1)}) fusion(pred[40,128]{0,1:T(8,128)(4,1)S(1)} %get-tuple-element.57, bf16[40,256]{1,0:T(8,128)(2,1)S(1)} %get-tuple-element.43, bf16[40,1,128,256]{3,2,1,0:T(8,128)(2,1)} %get-tuple-element.37, bf16[40,1,128,256]{3,2,1,0:T(8,128)(2,1)} %get-tuple-element.36, ...), kind=kLoop, calls=%fused_computation.26 | loop fusion | flops 2621440 | bytes 10531840 | tf_op jit(solution)/shard_map/jit(_where)/select_n | solution.py:60
  46.8 8.3 %all-gather.2.cloned.1.call-done = bf16[640,2048]{1,0:T(8,128)(2,1)} async-done(((bf16[80,2048]{1,0:T(8,128)(2,1)}), bf16[640,2048]{1,0:T(8,128)(2,1)}) %all-gather.2.cloned.1.call-update) | async-done | bytes 2621456 | tf_op jit(solution)/shard_map/all_gather | solution.py:85
  55.1 2.3 %convert_reduce_fusion = f32[640]{0:T(1024)S(1)} fusion(bf16[640,2048]{1,0:T(8,128)(2,1)} %all-gather.2.cloned.1.call-done), kind=kLoop, calls=%fused_computation.2 | loop fusion | flops 2620800 | bytes 2624000 | tf_op jit(solution)/shard_map/reduce_sum | solution.py:13
  57.4 0.2 copy-done.3
  57.6 0.8 fusion.3
  58.4 3.1 %fusion.25 = f32[3,640,256]{1,2,0:T(8,128)S(1)} fusion(bf16[3,2048,256]{2,1,0:T(8,128)(2,1)S(1)} %copy-done, bf16[640,2048]{1,0:T(8,128)(2,1)S(1)} %copy-done.3, f32[2048]{0:T(1024)S(1)} %copy-done.12, f32[2048]{0:T(1024)S(1)} %copy-done.13, f32[640]{0:T(1024)S(1)} %add_rsqrt_fusion, f32[640]{0:T(1024)S(1)} %broadcast_multiply_fusion), kind=kOutput, calls=%fused_computation.39 | convolution fusion | flops 2021130240 | bytes 7754752 | tf_op jit(solution)/shard_map/rd,cde->cre/dot_general | solution.py:86
  61.5 0.2 add_convert_fusion.1
  61.7 0.2 copy.64
  62.0 0.2 copy.63
  62.2 0.6 fusion.38
  62.8 0.4 copy-done.10
  63.2 2.0 fusion.74
  65.2 0.5 fusion.28
  65.7 0.7 copy-done.5
  66.4 2.4 %convolution_convert_fusion = bf16[640,2048]{1,0:T(8,128)(2,1)} fusion(bf16[640,256]{0,1:T(8,128)(2,1)S(1)} %bitcast.78, bf16[256,2048]{1,0:T(8,128)(2,1)S(1)} %copy-done.5), kind=kOutput, calls=%fused_computation.14 | convolution fusion | flops 672399360 | bytes 3997696 | tf_op jit(solution)/shard_map/dot_general | solution.py:107
  68.9 60.0 %all-reduce.2.cloned.1.call-done = bf16[40,2048]{1,0:T(8,128)(2,1)} async-done(((bf16[40,2048]{1,0:T(8,128)(2,1)}), bf16[40,2048]{1,0:T(8,128)(2,1)}) %all-reduce.2.cloned.1.call-update) | async-done | bytes 163856 | tf_op jit(solution)/shard_map/psum | solution.py:134
  128.8 1.0 fusion.37
  129.8 0.7 copy-done.8
  130.5 0.3 fusion.18
  130.8 0.5 broadcast.160
  131.3 1.3 reduce.1
  132.6 1.6 reshape.267
  134.3 7.4 %all-to-all-start = ((bf16[32,2,1024]{2,1,0:T(2,128)(2,1)}), bf16[32,2,1024]{2,1,0:T(2,128)(2,1)S(1)}, u32[]{:S(2)}, u32[]{:S(2)}) async-start(bf16[32,2,1024]{2,1,0:T(2,128)(2,1)} %reshape.267), calls=%async_computation.1 | async-start | bytes 262144 | tf_op jit(solution)/shard_map/all_to_all | solution.py:146
  141.7 2.6 %convolution_convert_fusion.1 = bf16[32,2,128,256]{3,0,2,1:T(8,128)(2,1)S(1)} fusion(bf16[40,1,128,256]{3,0,2,1:T(8,128)(2,1)S(1)} %copy-done.2, bf16[40,1,128,256]{3,0,2,1:T(8,128)(2,1)} %get-tuple-element.51, s32[16]{0:T(128)S(1)} %convert_add_fusion.1), kind=kOutput, calls=%fused_computation.16 | convolution fusion | flops 73400832 | bytes 9437248 | tf_op jit(solution)/shard_map/so,oklh->sklh/dot_general | solution.py:138
  144.3 4.4 %copy.72 = bf16[32,2,128,256]{3,2,1,0:T(8,128)(2,1)} copy(bf16[32,2,128,256]{3,0,2,1:T(8,128)(2,1)S(1)} %convolution_convert_fusion.1) | data formatting | bytes 8388608 | tf_op jit(solution)/shard_map/convert_element_type | solution.py:140
  148.7 7.4 %all-to-all-start.1 = ((bf16[32,2,128,256]{3,2,1,0:T(8,128)(2,1)}), bf16[32,2,128,256]{3,2,1,0:T(8,128)(2,1)}, u32[]{:S(2)}, u32[]{:S(2)}) async-start(bf16[32,2,128,256]{3,2,1,0:T(8,128)(2,1)} %copy.72), calls=%async_computation.2 | async-start | bytes 8388608 | tf_op jit(solution)/shard_map/all_to_all | solution.py:145
  156.2 1.6 fusion.7
  157.8 2.4 %copy.74 = bf16[24,2,128,256]{3,2,1,0:T(8,128)(2,1)} copy(bf16[24,2,128,256]{3,0,2,1:T(8,128)(2,1)S(1)} %fusion.7) | data formatting | bytes 6291456
  160.1 0.6 slice.71
  160.9 0.7 copy.116
  161.6 49.1 %all-to-all-done.1 = bf16[32,2,128,256]{3,2,1,0:T(8,128)(2,1)} async-done(((bf16[32,2,128,256]{3,2,1,0:T(8,128)(2,1)}), bf16[32,2,128,256]{3,2,1,0:T(8,128)(2,1)}, u32[]{:S(2)}, u32[]{:S(2)}) %all-to-all-start.1) | async-done | bytes 4194336 | tf_op jit(solution)/shard_map/all_to_all | solution.py:145
  210.8 1.1 copy.73
  211.9 1.8 add_convert_fusion.2
  213.7 4.8 %copy.120 = bf16[32,2,128,256]{3,2,1,0:T(8,128)(2,1)} copy(bf16[32,2,128,256]{3,2,1,0:T(8,128)(2,1)} %all-to-all-done.1) | data formatting | bytes 8388608
  (60 shorter events, 1.4 us)
Async XLA Ops:
  7.2 4.0 %copy-start = (bf16[3,2048,256]{2,1,0:T(8,128)(2,1)S(1)}, bf16[3,2048,256]{2,1,0:T(8,128)(2,1)}, u32[]{:S(2)}) copy-start(bf16[3,2048,256]{2,1,0:T(8,128)(2,1)} %param.20) | copy-start | bytes 9437188
  7.2 5.7 %copy-start.15 = (f32[3,256]{1,0:T(4,128)S(1)}, f32[3,256]{1,0:T(4,128)}, u32[]{:S(2)}) copy-start(f32[3,256]{1,0:T(4,128)} %param.21) | copy-start | bytes 9220
  7.2 47.9 %all-gather.2.cloned.1.call-start = ((), (), s32[]{:S(2)}) async-start(), calls=%async_computation.3 | async-start | bytes 2949120 | tf_op jit(solution)/shard_map/all_gather | solution.py:85
  7.9 120.9 %all-reduce.2.cloned.1.call-start = ((), (), s32[]{:S(2)}) async-start(), calls=%async_computation.5 | async-start | bytes 327680 | tf_op jit(solution)/shard_map/psum | solution.py:134
  31.1 4.6 %copy-start.4 = (bf16[256,2048]{1,0:T(8,128)(2,1)S(1)}, bf16[256,2048]{1,0:T(8,128)(2,1)}, u32[]{:S(2)}) copy-start(bf16[256,2048]{1,0:T(8,128)(2,1)} %param.22) | copy-start | bytes 3145732
  31.1 5.8 %copy-start.16 = (s32[16,1]{0,1:T(1,128)S(1)}, s32[16,1]{0,1:T(1,128)}, u32[]{:S(2)}) copy-start(s32[16,1]{0,1:T(1,128)} %param.16) | copy-start | bytes 196
  31.1 6.1 %copy-start.14 = (s32[1,640]{1,0:T(1,128)S(1)}, s32[1,640]{1,0:T(1,128)}, u32[]{:S(2)}) copy-start(s32[1,640]{1,0:T(1,128)} %param.13) | copy-start | bytes 7684
  36.6 175.2 %reduce-scatter.2.cloned.1.call-start = ((), (), s32[]{:S(2)}) async-start(), calls=%async_computation.4 | async-start | bytes 2949120 | tf_op jit(solution)/shard_map/reduce_scatter | solution.py:106
  46.8 11.7 %copy-start.12 = (f32[2048]{0:T(1024)S(1)}, f32[2048]{0:T(1024)}, u32[]{:S(2)}) copy-start(f32[2048]{0:T(1024)} %param.19) | copy-start | bytes 24580
  55.1 2.5 %copy-start.3 = (bf16[640,2048]{1,0:T(8,128)(2,1)S(1)}, bf16[640,2048]{1,0:T(8,128)(2,1)}, u32[]{:S(2)}) copy-start(bf16[640,2048]{1,0:T(8,128)(2,1)} %all-gather.2.cloned.1.call-done) | copy-start | bytes 7864324
  55.1 3.4 %copy-start.13 = (f32[2048]{0:T(1024)S(1)}, f32[2048]{0:T(1024)}, u32[]{:S(2)}) copy-start(f32[2048]{0:T(1024)} %param.18) | copy-start | bytes 24580
  62.2 1.0 copy-start.10
  65.2 1.2 copy-start.5
  66.4 62.4 %copy-start.6 = (bf16[40,2048]{1,0:T(8,128)(2,1)S(1)}, bf16[40,2048]{1,0:T(8,128)(2,1)}, u32[]{:S(2)}) copy-start(bf16[40,2048]{1,0:T(8,128)(2,1)} %param.14) | copy-start | bytes 491524
  66.4 62.4 %copy-start.11 = (f32[2048]{0:T(1024)S(1)}, f32[2048]{0:T(1024)}, u32[]{:S(2)}) copy-start(f32[2048]{0:T(1024)} %param.23) | copy-start | bytes 24580
  68.8 72.9 %copy-start.2 = (bf16[40,1,128,256]{3,0,2,1:T(8,128)(2,1)S(1)}, bf16[40,1,128,256]{3,0,2,1:T(8,128)(2,1)}, u32[]{:S(2)}) copy-start(bf16[40,1,128,256]{3,0,2,1:T(8,128)(2,1)} %get-tuple-element.50) | copy-start | bytes 7864324
  129.8 0.7 copy-start.8
  134.3 14.5 %all-to-all-start = ((bf16[32,2,1024]{2,1,0:T(2,128)(2,1)}), bf16[32,2,1024]{2,1,0:T(2,128)(2,1)S(1)}, u32[]{:S(2)}, u32[]{:S(2)}) async-start(bf16[32,2,1024]{2,1,0:T(2,128)(2,1)} %reshape.267), calls=%async_computation.1 | async-start | bytes 262144 | tf_op jit(solution)/shard_map/all_to_all | solution.py:146
  148.7 62.0 %all-to-all-start.1 = ((bf16[32,2,128,256]{3,2,1,0:T(8,128)(2,1)}), bf16[32,2,128,256]{3,2,1,0:T(8,128)(2,1)}, u32[]{:S(2)}, u32[]{:S(2)}) async-start(bf16[32,2,128,256]{3,2,1,0:T(8,128)(2,1)} %copy.72), calls=%async_computation.2 | async-start | bytes 8388608 | tf_op jit(solution)/shard_map/all_to_all | solution.py:145
  157.8 2.4 %copy-start.9 = (bf16[40,2048]{1,0:T(8,128)(2,1)S(1)}, bf16[40,2048]{1,0:T(8,128)(2,1)}, u32[]{:S(2)}) copy-start(bf16[40,2048]{1,0:T(8,128)(2,1)} %copy-done.8) | copy-start | bytes 491524
  160.1 51.7 %copy-start.7 = (bf16[80,2048]{1,0:T(8,128)(2,1)S(1)}, bf16[80,2048]{1,0:T(8,128)(2,1)}, u32[]{:S(2)}) copy-start(bf16[80,2048]{1,0:T(8,128)(2,1)} %param.12) | copy-start | bytes 983044
  213.7 4.9 %copy-start.1 = (bf16[3,2048,256]{2,1,0:T(8,128)(2,1)S(1)}, bf16[3,2048,256]{2,1,0:T(8,128)(2,1)}, u32[]{:S(2)}) copy-start(bf16[3,2048,256]{2,1,0:T(8,128)(2,1)} %param.20) | copy-start | bytes 9437188
Sparse Core Ops, SparseCore 0:
  9.8 45.1 all-gather.1
  58.0 70.8 all-reduce.1
  131.6 42.1 reduce-scatter.1
where the time goes:
time: 226 us; the launch traced here: 225 us
  waiting for transfers between devices  118 us (52%)
  local copies, waits for them, and re-layouts  34.1 us (15%)
  other arithmetic  24.3 us (11%)
  matrix products  19.4 us (9%)
  starting transfers between devices  15.1 us (7%)
  between operations  14.1 us (6%)
    psum x1, waiting for transfers between devices, on_device(): lax.psum(partial_value.astype(jnp.bfloat16), 'tp').astype(jnp.float32)  60 us
    all_to_all x1, waiting for transfers between devices, on_device(): lax.all_to_all(send_cache, 'rep', split_axis=0, concat_axis=0, tiled=True)  49.1 us
    unnamed x40, local copies, waits for them, and re-layouts  12.8 us
    select_n x1, other arithmetic, decode_partial(): new_values = jnp.where(written, value_new[:, None, :], cache[:, 1])  8.49 us
    all_gather x1, waiting for transfers between devices, on_device(): lax.all_gather(prompt_rows, 'tp', axis=0, tiled=True)  8.31 us
    all_to_all x1, starting transfers between devices, on_device(): lax.all_to_all(send_cache, 'rep', split_axis=0, concat_axis=0, tiled=True)  7.44 us
    all_to_all x1, starting transfers between devices, on_device(): lax.all_to_all(send_rows, 'rep', split_axis=0, concat_axis=0, tiled=True)  7.41 us
    slice x1, local copies, waits for them, and re-layouts, decode_partial(): old_keys = cache[:, 0].reshape(count, length, heads_here, HEAD_DIM)  5.54 us
  transfers between devices with their start and end apart: 5, of which 3 were waited for; matrix products, arithmetic and copies ran while one was open for 31% of the time, Pallas kernels for 0%

commit v1 on v0

--- a/solution.py
+++ b/solution.py
@@ -6,6 +6,14 @@
 HEAD_DIM = 128
 CAP = 1
 EPSILON = 1e-05
+
+
+def gather_by_exchange(shard, axis, dim):
+    size = lax.axis_size(axis)
+    repeats = [size if d == dim else 1 for d in range(shard.ndim)]
+    return lax.all_to_all(
+        jnp.tile(shard, repeats), axis, split_axis=dim, concat_axis=dim, tiled=True
+    )
 
 
 def layer_norm(values, norm_gain, norm_bias):
@@ -82,7 +90,7 @@
     leaving = migrate_to.shape[0]
     staying = decode_rows.shape[0] - leaving
     slot_count = rep_count * CAP
-    normed = layer_norm(lax.all_gather(prompt_rows, "tp", axis=0, tiled=True), norm_gain, norm_bias)
+    normed = layer_norm(gather_by_exchange(prompt_rows, "tp", 0), norm_gain, norm_bias)
     projected = jnp.einsum("rd,cde->cre", normed, qkv_weight, preferred_element_type=jnp.float32)
     total_rows = projected.shape[1]
     queries = (projected[0] + qkv_bias[0]).astype(jnp.bfloat16)

time: 226 us -> 230 us (1.018)
  waiting for transfers between devices: 118 us -> 99.9 us
  starting transfers between devices: 15.1 us -> 23.7 us
  other arithmetic: 24.3 us -> 32.7 us
  local copies, waits for them, and re-layouts: 34.1 us -> 40.3 us
    psum x1, waiting for transfers between devices: 60 us -> 33.5 us  [on_device(): lax.psum(partial_value.astype(jnp.bfloat16), 'tp').astype(jnp.float32)]
    all_to_all x0 -> x1, waiting for transfers between devices: none -> 17.3 us  [gather_by_exchange(): lax.all_to_all(jnp.tile(shard, repeats), axis, split_axis=dim, concat_axi...]
    all_to_all x0 -> x1, starting transfers between devices: none -> 8.61 us  [gather_by_exchange(): lax.all_to_all(jnp.tile(shard, repeats), axis, split_axis=dim, concat_axi...]
    all_gather x1 -> x0, waiting for transfers between devices: 8.31 us -> none  [on_device(): lax.all_gather(prompt_rows, 'tp', axis=0, tiled=True)]
    another operation x0 -> x1, local copies, waits for them, and re-layouts: none -> 2.94 us  [gather_by_exchange(): jnp.tile(shard, repeats)]
    convert_element_type x0 -> x1, other arithmetic: none -> 2.78 us  [layer_norm(): return (scaled * norm_gain + norm_bias).astype(jnp.bfloat16)]
    unnamed x40 -> x48, local copies, waits for them, and re-layouts: 12.8 us -> 10.7 us
  transfers between devices with their start and end apart: 5 -> 5, of which waited for: 3 -> 3; matrix products, arithmetic and copies ran while one was open for 31% -> 35% of each run, Pallas kernels for 0% -> 0%
where the time goes in v1:
time: 230 us; the launch traced here: 229 us
  waiting for transfers between devices  99.9 us (43%)
  local copies, waits for them, and re-layouts  40.3 us (18%)
  other arithmetic  32.7 us (14%)
  starting transfers between devices  23.7 us (10%)
  matrix products  18 us (8%)
  between operations  14.4 us (6%)
    all_to_all x1, waiting for transfers between devices, on_device(): lax.all_to_all(send_cache, 'rep', split_axis=0, concat_axis=0, tiled=True)  49.1 us
    psum x1, waiting for transfers between devices, on_device(): lax.psum(partial_value.astype(jnp.bfloat16), 'tp').astype(jnp.float32)  33.5 us
    all_to_all x1, waiting for transfers between devices, gather_by_exchange(): lax.all_to_all(jnp.tile(shard, repeats), axis, split_axis=dim, concat_axi...  17.3 us
    unnamed x48, local copies, waits for them, and re-layouts  10.7 us
    all_to_all x1, starting transfers between devices, gather_by_exchange(): lax.all_to_all(jnp.tile(shard, repeats), axis, split_axis=dim, concat_axi...  8.61 us
    select_n x1, other arithmetic, decode_partial(): new_values = jnp.where(written, value_new[:, None, :], cache[:, 1])  8.4 us
    all_to_all x1, starting transfers between devices, on_device(): lax.all_to_all(send_cache, 'rep', split_axis=0, concat_axis=0, tiled=True)  7.44 us
    all_to_all x1, starting transfers between devices, on_device(): lax.all_to_all(send_rows, 'rep', split_axis=0, concat_axis=0, tiled=True)  7.4 us
  transfers between devices with their start and end apart: 5, of which 3 were waited for; matrix products, arithmetic and copies ran while one was open for 35% of the time, Pallas kernels for 0%

profile of v1, /device:TPU:8, one launch (start us, length us, event | category | flops | bytes accessed | tf_op | source)
XLA Modules:
  0.0 229.0 jit_solution(17110308166304728449)
XLA Ops:
  7.2 2.9 %tile.2 = bf16[8,80,2048]{2,1,0:T(8,128)(2,1)} broadcast(bf16[80,2048]{1,0:T(8,128)(2,1)} %param.12), dimensions={1,2} | broadcast | bytes 2949120 | tf_op jit(solution)/shard_map/tile | solution.py:15
  10.1 8.6 %all-to-all-start = ((bf16[8,80,2048]{2,1,0:T(8,128)(2,1)}), bf16[8,80,2048]{2,1,0:T(8,128)(2,1)}, u32[]{:S(2)}, u32[]{:S(2)}) async-start(bf16[8,80,2048]{2,1,0:T(8,128)(2,1)} %tile.2), calls=%async_computation | async-start | bytes 5242880 | tf_op jit(solution)/shard_map/all_to_all | solution.py:14
  19.2 0.6 iota_compare_fusion.1
  19.9 0.7 convolution_bitcast_fusion
  20.6 0.7 fusion.65
  21.3 0.8 squeeze.31
  22.1 1.4 squeeze.30
  23.5 0.6 fusion.66
  24.1 1.5 multiply_reduce_fusion.1
  25.6 1.4 copy.68
  27.0 5.6 %fusion.64 = (bf16[40,1,128,256]{3,2,1,0:T(8,128)(2,1)}, bf16[40,1,128,256]{3,2,1,0:T(8,128)(2,1)}) fusion(bf16[40,2,128,256]{3,2,1,0:T(8,128)(2,1)} %param.17), kind=kLoop, calls=%fused_computation.112 | loop fusion | bytes 10485760 | tf_op jit(solution)/shard_map/slice | solution.py:39
  32.5 4.4 %copy.84 = bf16[40,1,128,256]{2,3,0,1:T(8,128)(2,1)} copy(bf16[40,1,128,256]{3,2,1,0:T(8,128)(2,1)} %get-tuple-element.36) | data formatting | bytes 5242880 | tf_op jit(solution)/shard_map/reshape;squeeze | solution.py:39
  36.9 2.5 %fusion.46 = f32[40,2,1,128]{3,2,1,0:T(1,128)S(1)} fusion(bf16[40,128,2,128]{1,3,2,0:T(8,128)(2,1)} %bitcast.85, bf16[40,2,128,1]{2,1,0,3:T(2,128)(2,1)S(1)} %get-tuple-element.49), kind=kOutput, calls=%fused_computation.77 | convolution fusion | flops 2621440 | bytes 2682880 | tf_op jit(solution)/shard_map/rhe,rlhe->rhl/dot_general | solution.py:43
  39.5 0.7 multiply_maximum_fusion
  40.4 1.3 fusion.58
  41.7 0.8 copy.70
  42.4 4.9 %reshape.296 = bf16[40,128,2,128]{3,2,1,0:T(2,128)(2,1)} reshape(bf16[40,1,128,256]{3,2,1,0:T(8,128)(2,1)} %get-tuple-element.37) | data formatting | bytes 5242880 | tf_op jit(solution)/shard_map/reshape;squeeze | solution.py:40
  47.3 0.8 fusion.52
  48.2 4.4 %fusion.8 = f32[40,2,1,128]{3,2,1,0:T(1,128)S(1)} fusion(bf16[40,2,128,1]{2,0,1,3:T(8,128)(2,1)S(1)} %fusion.52, bf16[40,128,2,128]{3,2,1,0:T(2,128)(2,1)} %reshape.296), kind=kOutput, calls=%fused_computation.18 | convolution fusion | flops 2621440 | bytes 2682880 | tf_op jit(solution)/shard_map/rhl,rlhe->rhe/dot_general | solution.py:60
  52.7 1.0 convolution_convert_fusion.2
  54.2 1.0 fusion.16
  55.3 8.4 %broadcast_select_fusion = (bf16[40,1,128,256]{3,0,2,1:T(8,128)(2,1)}, bf16[40,1,128,256]{3,0,2,1:T(8,128)(2,1)}) fusion(pred[40,128]{0,1:T(8,128)(4,1)S(1)} %copy-done.8, bf16[40,256]{1,0:T(8,128)(2,1)S(1)} %get-tuple-element.43, bf16[40,1,128,256]{3,2,1,0:T(8,128)(2,1)} %get-tuple-element.37, bf16[40,1,128,256]{3,2,1,0:T(8,128)(2,1)} %get-tuple-element.36, ...), kind=kLoop, calls=%fused_computation.21 | loop fusion | flops 2621440 | bytes 10531840 | tf_op jit(solution)/shard_map/jit(_where)/select_n | solution.py:68
  63.7 17.3 %all-to-all-done = bf16[8,80,2048]{2,1,0:T(8,128)(2,1)} async-done(((bf16[8,80,2048]{2,1,0:T(8,128)(2,1)}), bf16[8,80,2048]{2,1,0:T(8,128)(2,1)}, u32[]{:S(2)}, u32[]{:S(2)}) %all-to-all-start) | async-done | bytes 2621472 | tf_op jit(solution)/shard_map/all_to_all | solution.py:14
  81.0 2.2 convert_reduce_fusion
  83.2 2.6 %multiply_reduce_fusion = f32[8,80]{1,0:T(8,128)S(1)} fusion(bf16[8,80,2048]{2,1,0:T(8,128)(2,1)} %all-to-all-done, f32[8,80]{1,0:T(8,128)S(1)} %broadcast_multiply_fusion), kind=kLoop, calls=%fused_computation.8 | loop fusion | flops 5242240 | bytes 2626560 | tf_op jit(solution)/shard_map/reduce_sum | solution.py:22
  85.9 2.8 %fusion.4 = bf16[640,2048]{1,0:T(8,128)(2,1)S(1)} fusion(bf16[8,80,2048]{2,1,0:T(8,128)(2,1)} %all-to-all-done, f32[2048]{0:T(1024)S(1)} %copy-done.9, f32[2048]{0:T(1024)S(1)} %copy-done.11, f32[640]{0:T(1024)S(1)} %rsqrt.20, f32[640]{0:T(1024)S(1)} %div.38), kind=kLoop, calls=%fused_computation.7 | loop fusion | flops 7864320 | bytes 5264384 | tf_op jit(solution)/shard_map/convert_element_type | solution.py:24
  88.7 2.8 %fusion.18 = f32[3,640,256]{1,2,0:T(8,128)S(1)} fusion(bf16[3,2048,256]{2,1,0:T(8,128)(2,1)S(1)} %copy-done, bf16[640,2048]{1,0:T(8,128)(2,1)S(1)} %fusion.4), kind=kOutput, calls=%fused_computation.34 | convolution fusion | flops 2013265920 | bytes 7733248 | tf_op jit(solution)/shard_map/rd,cde->cre/dot_general | solution.py:94
  91.5 0.9 add_convert_fusion.1
  92.9 0.6 fusion.31
  93.5 4.0 %fusion.67 = (f32[2,640]{1,0:T(2,128)S(1)}, f32[2,640,640]{1,2,0:T(8,128)S(1)}) fusion(f32[2,640,640]{1,2,0:T(8,128)S(1)} %fusion.31, pred[640,640]{0,1:T(8,128)(4,1)} %fusion.16), kind=kOutput, calls=%fused_computation.115 | output fusion | flops 4915839 | bytes 6968320 | tf_op jit(solution)/shard_map/sub | solution.py:110
  98.1 0.7 copy-done.4
  98.8 2.4 %convolution_convert_fusion = bf16[640,2048]{1,0:T(8,128)(2,1)} fusion(bf16[640,256]{0,1:T(8,128)(2,1)S(1)} %bitcast.88, bf16[256,2048]{1,0:T(8,128)(2,1)S(1)} %copy-done.4), kind=kOutput, calls=%fused_computation.12 | convolution fusion | flops 672399360 | bytes 3997696 | tf_op jit(solution)/shard_map/dot_general | solution.py:115
  101.2 33.5 %all-reduce.2.cloned.1.call-done = bf16[40,2048]{1,0:T(8,128)(2,1)} async-done(((bf16[40,2048]{1,0:T(8,128)(2,1)}), bf16[40,2048]{1,0:T(8,128)(2,1)}) %all-reduce.2.cloned.1.call-update) | async-done | bytes 163856 | tf_op jit(solution)/shard_map/psum | solution.py:142
  134.7 1.0 fusion.30
  136.5 0.7 reduce.3
  137.2 0.7 reshape.297
  137.9 7.4 %all-to-all-start.1 = ((bf16[32,2,1024]{2,1,0:T(2,128)(2,1)}), bf16[32,2,1024]{2,1,0:T(2,128)(2,1)S(1)}, u32[]{:S(2)}, u32[]{:S(2)}) async-start(bf16[32,2,1024]{2,1,0:T(2,128)(2,1)} %reshape.297), calls=%async_computation.2 | async-start | bytes 262144 | tf_op jit(solution)/shard_map/all_to_all | solution.py:154
  145.4 2.6 %convolution_convert_fusion.1 = bf16[32,2,128,256]{3,0,2,1:T(8,128)(2,1)S(1)} fusion(bf16[40,1,128,256]{3,0,2,1:T(8,128)(2,1)S(1)} %copy-done.2, bf16[40,1,128,256]{3,0,2,1:T(8,128)(2,1)} %get-tuple-element.51, s32[16]{0:T(128)S(1)} %convert_add_fusion.1), kind=kOutput, calls=%fused_computation.14 | convolution fusion | flops 73400832 | bytes 9437248 | tf_op jit(solution)/shard_map/so,oklh->sklh/dot_general | solution.py:146
  148.0 4.4 %copy.72 = bf16[32,2,128,256]{3,2,1,0:T(8,128)(2,1)} copy(bf16[32,2,128,256]{3,0,2,1:T(8,128)(2,1)S(1)} %convolution_convert_fusion.1) | data formatting | bytes 8388608 | tf_op jit(solution)/shard_map/convert_element_type | solution.py:148
  152.4 7.4 %all-to-all-start.2 = ((bf16[32,2,128,256]{3,2,1,0:T(8,128)(2,1)}), bf16[32,2,128,256]{3,2,1,0:T(8,128)(2,1)}, u32[]{:S(2)}, u32[]{:S(2)}) async-start(bf16[32,2,128,256]{3,2,1,0:T(8,128)(2,1)} %copy.72), calls=%async_computation.3 | async-start | bytes 8388608 | tf_op jit(solution)/shard_map/all_to_all | solution.py:153
  159.8 1.6 fusion.5
  161.4 2.4 %copy.74 = bf16[24,2,128,256]{3,2,1,0:T(8,128)(2,1)} copy(bf16[24,2,128,256]{3,0,2,1:T(8,128)(2,1)S(1)} %fusion.5) | data formatting | bytes 6291456
  163.8 0.6 slice.71
  164.6 0.7 copy.116
  165.3 49.1 %all-to-all-done.2 = bf16[32,2,128,256]{3,2,1,0:T(8,128)(2,1)} async-done(((bf16[32,2,128,256]{3,2,1,0:T(8,128)(2,1)}), bf16[32,2,128,256]{3,2,1,0:T(8,128)(2,1)}, u32[]{:S(2)}, u32[]{:S(2)}) %all-to-all-start.2) | async-done | bytes 4194336 | tf_op jit(solution)/shard_map/all_to_all | solution.py:153
  214.5 1.1 copy.73
  215.5 1.8 add_convert_fusion.2
  217.3 4.8 %copy.120 = bf16[32,2,128,256]{3,2,1,0:T(8,128)(2,1)} copy(bf16[32,2,128,256]{3,2,1,0:T(8,128)(2,1)} %all-to-all-done.2) | data formatting | bytes 8388608
  (71 shorter events, 3.7 us)
Async XLA Ops:
  7.2 12.7 %copy-start = (bf16[3,2048,256]{2,1,0:T(8,128)(2,1)S(1)}, bf16[3,2048,256]{2,1,0:T(8,128)(2,1)}, u32[]{:S(2)}) copy-start(bf16[3,2048,256]{2,1,0:T(8,128)(2,1)} %param.20) | copy-start | bytes 9437188
  10.1 8.7 %copy-start.5 = (bf16[40,2048]{1,0:T(8,128)(2,1)S(1)}, bf16[40,2048]{1,0:T(8,128)(2,1)}, u32[]{:S(2)}) copy-start(bf16[40,2048]{1,0:T(8,128)(2,1)} %param.14) | copy-start | bytes 491524
  10.1 9.0 %copy-start.19 = (s32[40]{0:T(128)S(1)}, s32[40]{0:T(128)}, u32[]{:S(2)}) copy-start(s32[40]{0:T(128)} %param.15) | copy-start | bytes 484
  10.1 9.8 %copy-start.9 = (f32[2048]{0:T(1024)S(1)}, f32[2048]{0:T(1024)}, u32[]{:S(2)}) copy-start(f32[2048]{0:T(1024)} %param.19) | copy-start | bytes 24580
  10.1 9.8 %copy-start.10 = (f32[2048]{0:T(1024)S(1)}, f32[2048]{0:T(1024)}, u32[]{:S(2)}) copy-start(f32[2048]{0:T(1024)} %param.18) | copy-start | bytes 24580
  10.1 70.9 %all-to-all-start = ((bf16[8,80,2048]{2,1,0:T(8,128)(2,1)}), bf16[8,80,2048]{2,1,0:T(8,128)(2,1)}, u32[]{:S(2)}, u32[]{:S(2)}) async-start(bf16[8,80,2048]{2,1,0:T(8,128)(2,1)} %tile.2), calls=%async_computation | async-start | bytes 5242880 | tf_op jit(solution)/shard_map/all_to_all | solution.py:14
  18.7 4.8 %copy-start.18 = (f32[3,256]{1,0:T(4,128)S(1)}, f32[3,256]{1,0:T(4,128)}, u32[]{:S(2)}) copy-start(f32[3,256]{1,0:T(4,128)} %param.21) | copy-start | bytes 9220
  18.7 116.0 %all-reduce.2.cloned.1.call-start = ((), (), s32[]{:S(2)}) async-start(), calls=%async_computation.5 | async-start | bytes 327680 | tf_op jit(solution)/shard_map/psum | solution.py:142
  24.1 1.5 copy-start.15
  40.2 1.4 copy-start.14
  48.1 4.4 %copy-start.13 = (f32[1,256]{1,0:T(1,128)S(1)}, f32[1,256]{1,0:T(1,128)}, u32[]{:S(2)}) copy-start(f32[1,256]{1,0:T(1,128)} %get-tuple-element.52) | copy-start | bytes 3076
  48.1 4.5 %copy-start.3 = (bf16[256,2048]{1,0:T(8,128)(2,1)S(1)}, bf16[256,2048]{1,0:T(8,128)(2,1)}, u32[]{:S(2)}) copy-start(bf16[256,2048]{1,0:T(8,128)(2,1)} %param.22) | copy-start | bytes 3145732
  48.1 5.8 %copy-start.17 = (s32[1,640]{1,0:T(1,128)S(1)}, s32[1,640]{1,0:T(1,128)}, u32[]{:S(2)}) copy-start(s32[1,640]{1,0:T(1,128)} %param.13) | copy-start | bytes 7684
  48.1 5.8 %copy-start.20 = (s32[16,1]{0,1:T(1,128)S(1)}, s32[16,1]{0,1:T(1,128)}, u32[]{:S(2)}) copy-start(s32[16,1]{0,1:T(1,128)} %param.16) | copy-start | bytes 196
  48.1 7.1 %copy-start.8 = (pred[40,128]{0,1:T(8,128)(4,1)S(1)}, pred[40,128]{0,1:T(8,128)(4,1)}, u32[]{:S(2)}) copy-start(pred[40,128]{0,1:T(8,128)(4,1)} %get-tuple-element.57) | copy-start | bytes 15364
  53.7 161.9 %reduce-scatter.2.cloned.1.call-start = ((), (), s32[]{:S(2)}) async-start(), calls=%async_computation.4 | async-start | bytes 2949120 | tf_op jit(solution)/shard_map/reduce_scatter | solution.py:114
  63.7 22.2 %copy-start.11 = (f32[2048]{0:T(1024)S(1)}, f32[2048]{0:T(1024)}, u32[]{:S(2)}) copy-start(f32[2048]{0:T(1024)} %param.18) | copy-start | bytes 24580
  91.5 1.4 copy-start.16
  97.6 1.2 copy-start.4
  98.8 35.9 %copy-start.12 = (f32[2048]{0:T(1024)S(1)}, f32[2048]{0:T(1024)}, u32[]{:S(2)}) copy-start(f32[2048]{0:T(1024)} %param.23) | copy-start | bytes 24580
  101.2 44.2 %copy-start.2 = (bf16[40,1,128,256]{3,0,2,1:T(8,128)(2,1)S(1)}, bf16[40,1,128,256]{3,0,2,1:T(8,128)(2,1)}, u32[]{:S(2)}) copy-start(bf16[40,1,128,256]{3,0,2,1:T(8,128)(2,1)} %get-tuple-element.50) | copy-start | bytes 7864324
  137.9 14.5 %all-to-all-start.1 = ((bf16[32,2,1024]{2,1,0:T(2,128)(2,1)}), bf16[32,2,1024]{2,1,0:T(2,128)(2,1)S(1)}, u32[]{:S(2)}, u32[]{:S(2)}) async-start(bf16[32,2,1024]{2,1,0:T(2,128)(2,1)} %reshape.297), calls=%async_computation.2 | async-start | bytes 262144 | tf_op jit(solution)/shard_map/all_to_all | solution.py:154
  152.4 62.0 %all-to-all-start.2 = ((bf16[32,2,128,256]{3,2,1,0:T(8,128)(2,1)}), bf16[32,2,128,256]{3,2,1,0:T(8,128)(2,1)}, u32[]{:S(2)}, u32[]{:S(2)}) async-start(bf16[32,2,128,256]{3,2,1,0:T(8,128)(2,1)} %copy.72), calls=%async_computation.3 | async-start | bytes 8388608 | tf_op jit(solution)/shard_map/all_to_all | solution.py:153
  161.4 53.0 %copy-start.6 = (bf16[1,640,256]{1,2,0:T(8,128)(2,1)S(1)}, bf16[1,640,256]{1,2,0:T(8,128)(2,1)}, u32[]{:S(2)}) copy-start(bf16[1,640,256]{1,2,0:T(8,128)(2,1)} %get-tuple-element.39) | copy-start | bytes 983044
  163.8 51.7 %copy-start.7 = (bf16[80,2048]{1,0:T(8,128)(2,1)S(1)}, bf16[80,2048]{1,0:T(8,128)(2,1)}, u32[]{:S(2)}) copy-start(bf16[80,2048]{1,0:T(8,128)(2,1)} %param.12) | copy-start | bytes 983044
  217.3 4.9 %copy-start.1 = (bf16[3,2048,256]{2,1,0:T(8,128)(2,1)S(1)}, bf16[3,2048,256]{2,1,0:T(8,128)(2,1)}, u32[]{:S(2)}) copy-start(bf16[3,2048,256]{2,1,0:T(8,128)(2,1)} %param.20) | copy-start | bytes 9437188
Sparse Core Ops, SparseCore 0:
  53.8 80.9 all-reduce.1
  137.5 42.1 reduce-scatter.1
